TPU v7x, 32 devices: a whole 2x2x4 slice. The times are simulated.
32 devices in a mesh: clique: 8 (over z, core), shard: 4 (over y, x).
Axes of the slice: x: 2, y: 2, z: 4, core: 2. Of those that a mesh axis runs over, the one named last changes fastest.
Arguments:
- tables: float32 [3, 8, 4096, 128], P(None, 'clique', 'shard'), may hold values from 0.1 to 10
- up_map: int32 [2, 8, 4096], P(None, 'clique', 'shard'), may hold values from 0 to 4095, as said below
- down_map: int32 [2, 8, 4096], P(None, 'clique', 'shard'), may hold values from 0 to 4095, as said below
- parents: int32 [2, 8], replicated, may hold values from 0 to 7
Outputs:
- calibrated: float32 [3, 8, 4096, 128], P(None, 'clique', 'shard')
Inputs may be any that keep to these rules, and one draw needn't show every extreme that they name: For every edge and clique, of the 1024 blocks of one device exactly 256 name blocks in each range [k * 1024, (k + 1) * 1024). Every list of up_map and down_map names the same set of separator blocks; a named separator block is named by the same number of blocks of a clique in every list, a multiple of 1. For every edge and clique, of the 1024 blocks of one device exactly 256 name blocks in each range [k * 1024, (k + 1) * 1024). Every list of up_map and down_map names the same set of separator blocks; a named separator block is named by the same number of blocks of a clique in every list, a multiple of 1.
All inputs are finite; a program needn't handle non-finite values.
Results may differ from a plain program's by a relative error of at most 0.0003.
Values sent between devices are 32-bit elements; how exact they have to be, the bound alone decides.
No kernel may reach another device: no remote copies, remote signals or barrier semaphores. Data moves between devices by JAX's collectives and lax.ppermute only.
A program may use at most 64 MiB of HBM per device.

v0:
```python
import jax
import jax.numpy as jnp
from jax import lax
from jax.sharding import PartitionSpec as P

SEPB = 4096


def shards(tables, up_map, down_map, parents):
    shard_count = lax.axis_size("shard")
    clique_count = lax.axis_size("clique")
    block_count = tables.shape[2]
    lane_count = tables.shape[3]
    per_owner = SEPB // shard_count
    per_peer = block_count // shard_count
    sep_states = float(SEPB * lane_count)
    slot_ids = jnp.arange(per_owner, dtype=jnp.int32)

    def to_owners(potential, index_list):
        ordering = jnp.argsort(index_list // per_owner, stable=True)
        sent_rows = potential[ordering].reshape(shard_count, per_peer, lane_count)
        sent_slots = (index_list % per_owner)[ordering].reshape(shard_count, per_peer)
        arrived_rows, arrived_slots = (
            lax.all_to_all(sent_rows, "shard", split_axis=0, concat_axis=0, tiled=True),
            lax.all_to_all(sent_slots, "shard", split_axis=0, concat_axis=0, tiled=True),
        )
        one_hot = (arrived_slots.reshape(block_count)[:, None] == slot_ids[None, :]).astype(
            jnp.float32
        )
        message = jnp.dot(
            one_hot.T,
            arrived_rows.reshape(block_count, lane_count),
            precision=lax.Precision.HIGHEST,
            preferred_element_type=jnp.float32,
        )
        partial_sum = jnp.sum(message)
        total = lax.psum(partial_sum, "shard")
        return message * (sep_states / total)

    def fetch(owned_rows, index_list):
        gathered = lax.all_gather(owned_rows, "shard", axis=0, tiled=True)
        result = gathered[index_list]
        return result

    def route(owned_rows, mixing):
        pieces = owned_rows.reshape(clique_count, per_owner // clique_count, lane_count)
        combined = jnp.einsum(
            "oi,ixl->oxl",
            mixing,
            lax.all_to_all(pieces, "clique", split_axis=0, concat_axis=0, tiled=True),
            precision=lax.Precision.HIGHEST,
        )
        moved = lax.all_to_all(combined, "clique", split_axis=0, concat_axis=0, tiled=True)
        return moved.reshape(per_owner, lane_count)

    clique_ids = jnp.arange(clique_count, dtype=jnp.int32)
    current = [tables[0, 0], tables[1, 0], tables[2, 0]]
    previous = [tables[0, 0], tables[0, 0]]
    for edge in (1, 0):
        selector = (parents[edge][:, None] == clique_ids[None, :]).astype(jnp.float32)
        scaled = to_owners(current[edge + 1], up_map[edge, 0])
        previous[edge] = scaled
        incoming = jnp.exp(route(jnp.log(scaled), selector.T))
        current[edge] = current[edge] * fetch(incoming, down_map[edge, 0])
    for edge in (0, 1):
        selector = (parents[edge][:, None] == clique_ids[None, :]).astype(jnp.float32)
        fresh = to_owners(current[edge], down_map[edge, 0])
        from_parent = route(fresh, selector)
        update = from_parent / previous[edge]
        current[edge + 1] = current[edge + 1] * fetch(update, up_map[edge, 0])
    return jnp.stack(current)[:, None]


def solution(mesh):
    return jax.shard_map(
        shards,
        mesh=mesh,
        in_specs=(
            P(None, "clique", "shard", None),
            P(None, "clique", "shard"),
            P(None, "clique", "shard"),
            P(),
        ),
        out_specs=P(None, "clique", "shard", None),
        check_vma=False,
    )
```

profile of v0, /device:TPU:0, one launch (start us, length us, event | category | flops | bytes accessed | tf_op | source)
XLA Modules:
  0.0 467.1 jit_solution(16538825504890834248)
XLA Ops:
  11.6 8.8 %gather_fusion.1 = s32[1024]{0:T(1024)} fusion(s32[1024]{0:T(1024)S(1)} %get-tuple-element.30, s32[1024]{0:T(1024)S(1)} %fusion.17), kind=kCustom, calls=%fused_computation.1 | custom fusion | bytes 12288 | tf_op jit(solution)/shard_map/gather | solution.py:22
  30.3 10.1 %all_to_all.96 = f32[4,256,128]{2,1,0:T(8,128)S(1)} all-to-all(f32[4,256,128]{2,1,0:T(8,128)S(1)} %bitcast.91), channel_id=1, replica_groups=mesh['clique'=8,'shard'=4] {'shard'}, dimensions={0} | all-to-all | bytes 1048576 | tf_op jit(solution)/shard_map/all_to_all | solution.py:24
  44.7 9.0 %psum.28 = f32[]{:T(128)} all-reduce(f32[]{:T(128)} %get-tuple-element.34), channel_id=1, replica_groups=mesh['clique'=8,'shard'=4] {'shard'}, use_global_device_ids=true, to_apply=%region_3.4 | all-reduce | flops 1 | bytes 8 | tf_op jit(solution)/shard_map/psum | solution.py:37
  60.2 15.3 %all-to-all-done.3 = f32[8,128,128]{2,1,0:T(8,128)S(1)} async-done(((f32[8,128,128]{2,1,0:T(8,128)}), f32[8,128,128]{2,1,0:T(8,128)S(1)}, u32[]{:S(2)}, u32[]{:S(2)}) %all-to-all-start.3) | async-done | bytes 524320 | tf_op jit(solution)/shard_map/all_to_all | solution.py:50
  76.3 17.7 %all_to_all.97 = f32[8,128,128]{2,1,0:T(8,128)S(1)} all-to-all(f32[8,128,128]{2,1,0:T(8,128)S(1)} %copy.27), channel_id=1, replica_groups=mesh['clique'=8,'shard'=4] {'clique'}, dimensions={0} | all-to-all | bytes 1048576 | tf_op jit(solution)/shard_map/all_to_all | solution.py:53
  99.3 8.8 %gather_fusion = s32[1024]{0:T(1024)} fusion(s32[1024]{0:T(1024)S(1)} %get-tuple-element.28, s32[1024]{0:T(1024)S(1)} %fusion.16), kind=kCustom, calls=%fused_computation | custom fusion | bytes 12288 | tf_op jit(solution)/shard_map/gather | solution.py:22
  111.4 17.2 %all-gather.5.cloned.1.call-done = f32[4096,128]{1,0:T(8,128)} async-done(((f32[1024,128]{1,0:T(8,128)}), f32[4096,128]{1,0:T(8,128)}) %all-gather.5.cloned.1.call-update) | async-done | bytes 2097168 | tf_op jit(solution)/shard_map/all_gather | solution.py:41
  135.9 11.0 %all_to_all.98 = f32[4,256,128]{2,1,0:T(8,128)S(1)} all-to-all(f32[4,256,128]{2,1,0:T(8,128)S(1)} %bitcast.94), channel_id=1, replica_groups=mesh['clique'=8,'shard'=4] {'shard'}, dimensions={0} | all-to-all | bytes 1048576 | tf_op jit(solution)/shard_map/all_to_all | solution.py:24
  151.2 9.0 %psum.29 = f32[]{:T(128)} all-reduce(f32[]{:T(128)} %get-tuple-element.36), channel_id=1, replica_groups=mesh['clique'=8,'shard'=4] {'shard'}, use_global_device_ids=true, to_apply=%region_5.6 | all-reduce | flops 1 | bytes 8 | tf_op jit(solution)/shard_map/psum | solution.py:37
  161.0 19.7 %all_to_all.99 = f32[8,128,128]{2,1,0:T(8,128)S(1)} all-to-all(f32[8,128,128]{2,1,0:T(8,128)S(1)} %bitcast.90), channel_id=1, replica_groups=mesh['clique'=8,'shard'=4] {'clique'}, dimensions={0} | all-to-all | bytes 1048576 | tf_op jit(solution)/shard_map/all_to_all | solution.py:50
  181.5 17.7 %all_to_all.100 = f32[8,128,128]{2,1,0:T(8,128)S(1)} all-to-all(f32[8,128,128]{2,1,0:T(8,128)S(1)} %copy.30), channel_id=1, replica_groups=mesh['clique'=8,'shard'=4] {'clique'}, dimensions={0} | all-to-all | bytes 1048576 | tf_op jit(solution)/shard_map/all_to_all | solution.py:53
  204.6 8.8 %gather_fusion.6 = s32[1024]{0:T(1024)} fusion(s32[1024]{0:T(1024)S(1)} %get-tuple-element.26, s32[1024]{0:T(1024)S(1)} %fusion.18), kind=kCustom, calls=%fused_computation.6 | custom fusion | bytes 12288 | tf_op jit(solution)/shard_map/gather | solution.py:22
  216.7 17.2 %all-gather.7.cloned.1.call-done = f32[4096,128]{1,0:T(8,128)} async-done(((f32[1024,128]{1,0:T(8,128)}), f32[4096,128]{1,0:T(8,128)}) %all-gather.7.cloned.1.call-update) | async-done | bytes 2097168 | tf_op jit(solution)/shard_map/all_gather | solution.py:41
  244.6 12.1 %all_to_all.101 = f32[4,256,128]{2,1,0:T(8,128)S(1)} all-to-all(f32[4,256,128]{2,1,0:T(8,128)} %bitcast.92), channel_id=1, replica_groups=mesh['clique'=8,'shard'=4] {'shard'}, dimensions={0} | all-to-all | bytes 1048576 | tf_op jit(solution)/shard_map/all_to_all | solution.py:24
  261.7 9.0 %psum.30 = f32[]{:T(128)} all-reduce(f32[]{:T(128)} %get-tuple-element.38), channel_id=1, replica_groups=mesh['clique'=8,'shard'=4] {'shard'}, use_global_device_ids=true, to_apply=%region_8.9 | all-reduce | flops 1 | bytes 8 | tf_op jit(solution)/shard_map/psum | solution.py:37
  272.5 19.9 %all_to_all.102 = f32[8,128,128]{2,1,0:T(8,128)S(1)} all-to-all(f32[8,128,128]{2,1,0:T(8,128)S(1)} %bitcast.88), channel_id=1, replica_groups=mesh['clique'=8,'shard'=4] {'clique'}, dimensions={0} | all-to-all | bytes 1048576 | tf_op jit(solution)/shard_map/all_to_all | solution.py:50
  293.1 17.7 %all_to_all.103 = f32[8,128,128]{2,1,0:T(8,128)S(1)} all-to-all(f32[8,128,128]{2,1,0:T(8,128)S(1)} %copy.32), channel_id=1, replica_groups=mesh['clique'=8,'shard'=4] {'clique'}, dimensions={0} | all-to-all | bytes 1048576 | tf_op jit(solution)/shard_map/all_to_all | solution.py:53
  316.2 8.8 %gather_fusion.9 = s32[1024]{0:T(1024)} fusion(s32[1024]{0:T(1024)S(1)} %get-tuple-element.24, s32[1024]{0:T(1024)S(1)} %fusion.19), kind=kCustom, calls=%fused_computation.9 | custom fusion | bytes 12288 | tf_op jit(solution)/shard_map/gather | solution.py:22
  328.3 17.1 %all-gather.9.cloned.1.call-done = f32[4096,128]{1,0:T(8,128)} async-done(((f32[1024,128]{1,0:T(8,128)}), f32[4096,128]{1,0:T(8,128)}) %all-gather.9.cloned.1.call-update) | async-done | bytes 2097168 | tf_op jit(solution)/shard_map/all_gather | solution.py:41
  355.0 11.0 %all_to_all.104 = f32[4,256,128]{2,1,0:T(8,128)S(1)} all-to-all(f32[4,256,128]{2,1,0:T(8,128)S(1)} %bitcast.93), channel_id=1, replica_groups=mesh['clique'=8,'shard'=4] {'shard'}, dimensions={0} | all-to-all | bytes 1048576 | tf_op jit(solution)/shard_map/all_to_all | solution.py:24
  370.3 9.0 %psum.31 = f32[]{:T(128)} all-reduce(f32[]{:T(128)} %get-tuple-element.40), channel_id=1, replica_groups=mesh['clique'=8,'shard'=4] {'shard'}, use_global_device_ids=true, to_apply=%region_11.12 | all-reduce | flops 1 | bytes 8 | tf_op jit(solution)/shard_map/psum | solution.py:37
  379.9 19.9 %all_to_all.105 = f32[8,128,128]{2,1,0:T(8,128)S(1)} all-to-all(f32[8,128,128]{2,1,0:T(8,128)S(1)} %bitcast.89), channel_id=1, replica_groups=mesh['clique'=8,'shard'=4] {'clique'}, dimensions={0} | all-to-all | bytes 1048576 | tf_op jit(solution)/shard_map/all_to_all | solution.py:50
  400.6 17.7 %all_to_all.106 = f32[8,128,128]{2,1,0:T(8,128)S(1)} all-to-all(f32[8,128,128]{2,1,0:T(8,128)S(1)} %copy.34), channel_id=1, replica_groups=mesh['clique'=8,'shard'=4] {'clique'}, dimensions={0} | all-to-all | bytes 1048576 | tf_op jit(solution)/shard_map/all_to_all | solution.py:53
  419.3 33.2 %all-gather.11.cloned.1.call-done = f32[4096,128]{1,0:T(8,128)} async-done(((f32[1024,128]{1,0:T(8,128)}), f32[4096,128]{1,0:T(8,128)}) %all-gather.11.cloned.1.call-update) | async-done | bytes 2097168 | tf_op jit(solution)/shard_map/all_gather | solution.py:41
  (96 shorter events, 105.0 us)
Async XLA Ops:
  11.6 14.0 %copy-start = (f32[3,1,1024,128]{3,2,1,0:T(8,128)S(1)}, f32[3,1,1024,128]{3,2,1,0:T(8,128)}, u32[]{:S(2)}) copy-start(f32[3,1,1024,128]{3,2,1,0:T(8,128)} %param.4) | copy-start | bytes 4718596
  20.5 9.9 %all-to-all-start.1 = ((s32[4,1,256]{2,1,0:T(1,128)}), s32[4,1,256]{2,1,0:T(1,128)S(1)}, u32[]{:S(2)}, u32[]{:S(2)}) async-start(s32[4,1,256]{2,1,0:T(1,128)} %bitcast.10), calls=%async_computation.1 | async-start | bytes 8192 | tf_op jit(solution)/shard_map/all_to_all | solution.py:25
  40.5 19.7 %copy-start.9 = (s32[2,8]{1,0:T(2,128)S(1)}, s32[2,8]{1,0:T(2,128)}, u32[]{:S(2)}) copy-start(s32[2,8]{1,0:T(2,128)} %param.7) | copy-start | bytes 196
  44.7 31.6 %copy-start.3 = (f32[1024,128]{1,0:T(8,128)}, f32[1024,128]{1,0:T(8,128)S(1)}, u32[]{:S(2)}) copy-start(f32[1024,128]{1,0:T(8,128)S(1)} %get-tuple-element.35) | copy-start | bytes 1572868
  55.2 20.2 %all-to-all-start.3 = ((f32[8,128,128]{2,1,0:T(8,128)}), f32[8,128,128]{2,1,0:T(8,128)S(1)}, u32[]{:S(2)}, u32[]{:S(2)}) async-start(f32[8,128,128]{2,1,0:T(8,128)} %bitcast.15), calls=%async_computation.3 | async-start | bytes 1048576 | tf_op jit(solution)/shard_map/all_to_all | solution.py:50
  60.1 68.5 %all-gather.5.cloned.1.call-start = ((), (), s32[]{:S(2)}) async-start(), calls=%async_computation.16 | async-start | bytes 2621440 | tf_op jit(solution)/shard_map/all_gather | solution.py:41
  99.3 12.1 %copy-start.7 = (s32[2,1,1024]{2,1,0:T(1,128)S(1)}, s32[2,1,1024]{2,1,0:T(1,128)}, u32[]{:S(2)}) copy-start(s32[2,1,1024]{2,1,0:T(1,128)} %param.6) | copy-start | bytes 24580
  108.1 27.8 %all-to-all-start = ((s32[4,1,256]{2,1,0:T(1,128)}), s32[4,1,256]{2,1,0:T(1,128)S(1)}, u32[]{:S(2)}, u32[]{:S(2)}) async-start(s32[4,1,256]{2,1,0:T(1,128)} %bitcast.4), calls=%async_computation | async-start | bytes 8192 | tf_op jit(solution)/shard_map/all_to_all | solution.py:25
  111.3 122.6 %all-gather.7.cloned.1.call-start = ((), (), s32[]{:S(2)}) async-start(), calls=%async_computation.17 | async-start | bytes 2621440 | tf_op jit(solution)/shard_map/all_gather | solution.py:41
  151.2 30.4 %copy-start.5 = (f32[1024,128]{1,0:T(8,128)}, f32[1024,128]{1,0:T(8,128)S(1)}, u32[]{:S(2)}) copy-start(f32[1024,128]{1,0:T(8,128)S(1)} %get-tuple-element.37) | copy-start | bytes 1572868
  213.4 31.2 %all-to-all-start.8 = ((s32[4,1,256]{2,1,0:T(1,128)}), s32[4,1,256]{2,1,0:T(1,128)S(1)}, u32[]{:S(2)}, u32[]{:S(2)}) async-start(s32[4,1,256]{2,1,0:T(1,128)} %bitcast.30), calls=%async_computation.8 | async-start | bytes 8192 | tf_op jit(solution)/shard_map/all_to_all | solution.py:25
  216.7 128.8 %all-gather.9.cloned.1.call-start = ((), (), s32[]{:S(2)}) async-start(), calls=%async_computation.18 | async-start | bytes 2621440 | tf_op jit(solution)/shard_map/all_gather | solution.py:41
  272.4 38.4 %copy-start.6 = (f32[1024,128]{1,0:T(8,128)S(1)}, f32[1024,128]{1,0:T(8,128)}, u32[]{:S(2)}) copy-start(f32[1024,128]{1,0:T(8,128)} %copy-done.5) | copy-start | bytes 1572868
  316.2 12.1 %copy-start.8 = (s32[2,1,1024]{2,1,0:T(1,128)S(1)}, s32[2,1,1024]{2,1,0:T(1,128)}, u32[]{:S(2)}) copy-start(s32[2,1,1024]{2,1,0:T(1,128)} %param.5) | copy-start | bytes 24580
  325.0 30.0 %all-to-all-start.12 = ((s32[4,1,256]{2,1,0:T(1,128)}), s32[4,1,256]{2,1,0:T(1,128)S(1)}, u32[]{:S(2)}, u32[]{:S(2)}) async-start(s32[4,1,256]{2,1,0:T(1,128)} %bitcast.43), calls=%async_computation.12 | async-start | bytes 8192 | tf_op jit(solution)/shard_map/all_to_all | solution.py:25
  328.2 124.2 %all-gather.11.cloned.1.call-start = ((), (), s32[]{:S(2)}) async-start(), calls=%async_computation.19 | async-start | bytes 2621440 | tf_op jit(solution)/shard_map/all_gather | solution.py:41
  379.9 38.4 %copy-start.4 = (f32[1024,128]{1,0:T(8,128)S(1)}, f32[1024,128]{1,0:T(8,128)}, u32[]{:S(2)}) copy-start(f32[1024,128]{1,0:T(8,128)} %copy-done.3) | copy-start | bytes 1572868
  419.2 38.8 %copy-start.1 = (f32[1024,128]{1,0:T(8,128)S(1)}, f32[1024,128]{1,0:T(8,128)}, u32[]{:S(2)}) copy-start(f32[1024,128]{1,0:T(8,128)} %gather_fusion.5) | copy-start | bytes 1572868
  419.3 38.8 %copy-start.2 = (f32[1024,128]{1,0:T(8,128)S(1)}, f32[1024,128]{1,0:T(8,128)}, u32[]{:S(2)}) copy-start(f32[1024,128]{1,0:T(8,128)} %gather_fusion.8) | copy-start | bytes 1572868
Sparse Core Ops, SparseCore 0:
  95.1 33.5 all-gather.4
  200.3 33.5 all-gather.6
  311.9 33.5 all-gather.8
  419.4 33.0 all-gather.10
where the time goes:
time: 468 us; the launch traced here: 467 us
  blocking collectives  211 us (45%)
  waiting for transfers between devices  102 us (22%)
  local copies, waits for them, and re-layouts  71.8 us (15%)
  other arithmetic  26.1 us (6%)
  matrix products  20.5 us (4%)
  starting transfers between devices  19.9 us (4%)
  between operations  16.1 us (3%)
    all_gather x4, waiting for transfers between devices, fetch(): gathered = lax.all_gather(owned_rows, 'shard', axis=0, tiled=True)  84.7 us
    all_to_all x4, blocking collectives, route(): lax.all_to_all(combined, 'clique', split_axis=0, concat_axis=0, tiled=True)  70.9 us
    all_to_all x3, blocking collectives, route(): lax.all_to_all(pieces, 'clique', split_axis=0, concat_axis=0, tiled=True)  59.5 us
    all_to_all x4, blocking collectives, to_owners(): lax.all_to_all(sent_rows, 'shard', split_axis=0, concat_axis=0, tiled=True)  44.3 us
    psum x4, blocking collectives, to_owners(): total = lax.psum(partial_sum, 'shard')  36 us
    gather x4, local copies, waits for them, and re-layouts, to_owners(): (index_list % per_owner)[ordering].reshape(shard_count, per_peer)  35.3 us
    gather x4, local copies, waits for them, and re-layouts, fetch(): result = gathered[index_list]  21.2 us
    dot_general x4, matrix products, to_owners(): jnp.dot(one_hot.T, arrived_rows.reshape(block_count, lane_count), precisi...  17.8 us
  transfers between devices with their start and end apart: 9, of which 6 were waited for; matrix products, arithmetic and copies ran while one was open for 15% of the time, Pallas kernels for 0%

commit v1 on v0

--- a/solution.py
+++ b/solution.py
@@ -38,7 +38,9 @@
         return message * (sep_states / total)
 
     def fetch(owned_rows, index_list):
-        gathered = lax.all_gather(owned_rows, "shard", axis=0, tiled=True)
+        gathered = jnp.concatenate(
+            lax.all_to_all(jnp.stack([owned_rows] * lax.axis_size("shard")), "shard", 0, 0), axis=0
+        )
         result = gathered[index_list]
         return result
 

time: 468 us -> 437 us (0.934)
  waiting for transfers between devices: 102 us -> 75.3 us
  starting transfers between devices: 19.9 us -> 34.2 us
  between operations: 16.1 us -> 2.99 us
    all_gather x4 -> x0, waiting for transfers between devices: 84.7 us -> none  [fetch(): gathered = lax.all_gather(owned_rows, 'shard', axis=0, tiled=True)]
    all_to_all x0 -> x4, waiting for transfers between devices: none -> 59.2 us  [fetch(): lax.all_to_all(jnp.stack([owned_rows] * lax.axis_size('shard')), 'shard',...]
    all_to_all x0 -> x4, starting transfers between devices: none -> 14.4 us  [fetch(): lax.all_to_all(jnp.stack([owned_rows] * lax.axis_size('shard')), 'shard',...]
    gather x4, local copies, waits for them, and re-layouts: 21.2 us -> 14.8 us  [fetch(): result = gathered[index_list]]
    another operation x0 -> x4, local copies, waits for them, and re-layouts: none -> 5.95 us  [fetch(): jnp.stack([owned_rows] * lax.axis_size('shard'))]
where the time goes in v1:
time: 437 us; the launch traced here: 435 us
  blocking collectives  208 us (48%)
  waiting for transfers between devices  75.3 us (17%)
  local copies, waits for them, and re-layouts  69.8 us (16%)
  starting transfers between devices  34.2 us (8%)
  other arithmetic  25.4 us (6%)
  matrix products  19.8 us (5%)
    all_to_all x4, blocking collectives, route(): lax.all_to_all(combined, 'clique', split_axis=0, concat_axis=0, tiled=True)  70.9 us
    all_to_all x4, waiting for transfers between devices, fetch(): lax.all_to_all(jnp.stack([owned_rows] * lax.axis_size('shard')), 'shard',...  59.2 us
    all_to_all x3, blocking collectives, route(): lax.all_to_all(pieces, 'clique', split_axis=0, concat_axis=0, tiled=True)  55.5 us
    all_to_all x4, blocking collectives, to_owners(): lax.all_to_all(sent_rows, 'shard', split_axis=0, concat_axis=0, tiled=True)  45.4 us
    psum x4, blocking collectives, to_owners(): total = lax.psum(partial_sum, 'shard')  35.9 us
    gather x4, local copies, waits for them, and re-layouts, to_owners(): (index_list % per_owner)[ordering].reshape(shard_count, per_peer)  35.3 us
    sort x4, other arithmetic, to_owners(): ordering = jnp.argsort(index_list // per_owner, stable=True)  17.5 us
    dot_general x4, matrix products, to_owners(): jnp.dot(one_hot.T, arrived_rows.reshape(block_count, lane_count), precisi...  17 us
  transfers between devices with their start and end apart: 9, of which 6 were waited for; matrix products, arithmetic and copies ran while one was open for 15% of the time, Pallas kernels for 0%

profile of v1, /device:TPU:0, one launch (start us, length us, event | category | flops | bytes accessed | tf_op | source)
XLA Modules:
  0.0 435.2 jit_solution(1123531803942842145)
XLA Ops:
  5.1 8.8 %gather_fusion.1 = s32[1024]{0:T(1024)} fusion(s32[1024]{0:T(1024)S(1)} %get-tuple-element.30, s32[1024]{0:T(1024)S(1)} %fusion.17), kind=kCustom, calls=%fused_computation.1 | custom fusion | bytes 12288 | tf_op jit(solution)/shard_map/gather | solution.py:22
  23.8 11.2 %all_to_all.116 = f32[4,256,128]{2,1,0:T(8,128)S(1)} all-to-all(f32[4,256,128]{2,1,0:T(8,128)S(1)} %bitcast.99), channel_id=1, replica_groups=mesh['clique'=8,'shard'=4] {'shard'}, dimensions={0} | all-to-all | bytes 1048576 | tf_op jit(solution)/shard_map/all_to_all | solution.py:24
  39.2 9.0 %psum.28 = f32[]{:T(128)} all-reduce(f32[]{:T(128)} %get-tuple-element.34), channel_id=1, replica_groups=mesh['clique'=8,'shard'=4] {'shard'}, use_global_device_ids=true, to_apply=%region_3.4 | all-reduce | flops 1 | bytes 8 | tf_op jit(solution)/shard_map/psum | solution.py:37
  54.6 15.3 %all-to-all-done.3 = f32[8,128,128]{2,1,0:T(8,128)S(1)} async-done(((f32[8,128,128]{2,1,0:T(8,128)}), f32[8,128,128]{2,1,0:T(8,128)S(1)}, u32[]{:S(2)}, u32[]{:S(2)}) %all-to-all-start.3) | async-done | bytes 524320 | tf_op jit(solution)/shard_map/all_to_all | solution.py:52
  70.8 17.7 %all_to_all.117 = f32[8,128,128]{2,1,0:T(8,128)S(1)} all-to-all(f32[8,128,128]{2,1,0:T(8,128)S(1)} %copy.27), channel_id=1, replica_groups=mesh['clique'=8,'shard'=4] {'clique'}, dimensions={0} | all-to-all | bytes 1048576 | tf_op jit(solution)/shard_map/all_to_all | solution.py:55
  98.1 8.8 %gather_fusion = s32[1024]{0:T(1024)} fusion(s32[1024]{0:T(1024)S(1)} %get-tuple-element.28, s32[1024]{0:T(1024)S(1)} %fusion.16), kind=kCustom, calls=%fused_computation | custom fusion | bytes 12288 | tf_op jit(solution)/shard_map/gather | solution.py:22
  107.0 11.5 %all-to-all-done.5 = f32[4,1024,128]{2,1,0:T(8,128)S(1)} async-done(((f32[4,1024,128]{2,1,0:T(8,128)}), f32[4,1024,128]{2,1,0:T(8,128)S(1)}, u32[]{:S(2)}, u32[]{:S(2)}) %all-to-all-start.5) | async-done | bytes 2097184 | tf_op jit(solution)/shard_map/all_to_all | solution.py:42
  128.5 11.4 %all_to_all.118 = f32[4,256,128]{2,1,0:T(8,128)S(1)} all-to-all(f32[4,256,128]{2,1,0:T(8,128)S(1)} %bitcast.102), channel_id=1, replica_groups=mesh['clique'=8,'shard'=4] {'shard'}, dimensions={0} | all-to-all | bytes 1048576 | tf_op jit(solution)/shard_map/all_to_all | solution.py:24
  144.1 9.0 %psum.29 = f32[]{:T(128)} all-reduce(f32[]{:T(128)} %get-tuple-element.36), channel_id=1, replica_groups=mesh['clique'=8,'shard'=4] {'shard'}, use_global_device_ids=true, to_apply=%region_5.6 | all-reduce | flops 1 | bytes 8 | tf_op jit(solution)/shard_map/psum | solution.py:37
  153.9 18.4 %all_to_all.119 = f32[8,128,128]{2,1,0:T(8,128)S(1)} all-to-all(f32[8,128,128]{2,1,0:T(8,128)S(1)} %bitcast.98), channel_id=1, replica_groups=mesh['clique'=8,'shard'=4] {'clique'}, dimensions={0} | all-to-all | bytes 1048576 | tf_op jit(solution)/shard_map/all_to_all | solution.py:52
  173.2 17.7 %all_to_all.120 = f32[8,128,128]{2,1,0:T(8,128)S(1)} all-to-all(f32[8,128,128]{2,1,0:T(8,128)S(1)} %copy.30), channel_id=1, replica_groups=mesh['clique'=8,'shard'=4] {'clique'}, dimensions={0} | all-to-all | bytes 1048576 | tf_op jit(solution)/shard_map/all_to_all | solution.py:55
  200.5 8.8 %gather_fusion.6 = s32[1024]{0:T(1024)} fusion(s32[1024]{0:T(1024)S(1)} %get-tuple-element.26, s32[1024]{0:T(1024)S(1)} %fusion.18), kind=kCustom, calls=%fused_computation.6 | custom fusion | bytes 12288 | tf_op jit(solution)/shard_map/gather | solution.py:22
  209.3 11.5 %all-to-all-done.9 = f32[4,1024,128]{2,1,0:T(8,128)S(1)} async-done(((f32[4,1024,128]{2,1,0:T(8,128)}), f32[4,1024,128]{2,1,0:T(8,128)S(1)}, u32[]{:S(2)}, u32[]{:S(2)}) %all-to-all-start.9) | async-done | bytes 2097184 | tf_op jit(solution)/shard_map/all_to_all | solution.py:42
  232.2 11.4 %all_to_all.121 = f32[4,256,128]{2,1,0:T(8,128)S(1)} all-to-all(f32[4,256,128]{2,1,0:T(8,128)S(1)} %bitcast.100), channel_id=1, replica_groups=mesh['clique'=8,'shard'=4] {'shard'}, dimensions={0} | all-to-all | bytes 1048576 | tf_op jit(solution)/shard_map/all_to_all | solution.py:24
  247.9 9.0 %psum.30 = f32[]{:T(128)} all-reduce(f32[]{:T(128)} %get-tuple-element.38), channel_id=1, replica_groups=mesh['clique'=8,'shard'=4] {'shard'}, use_global_device_ids=true, to_apply=%region_8.9 | all-reduce | flops 1 | bytes 8 | tf_op jit(solution)/shard_map/psum | solution.py:37
  257.5 18.5 %all_to_all.122 = f32[8,128,128]{2,1,0:T(8,128)S(1)} all-to-all(f32[8,128,128]{2,1,0:T(8,128)S(1)} %bitcast.96), channel_id=1, replica_groups=mesh['clique'=8,'shard'=4] {'clique'}, dimensions={0} | all-to-all | bytes 1048576 | tf_op jit(solution)/shard_map/all_to_all | solution.py:52
  276.9 17.7 %all_to_all.123 = f32[8,128,128]{2,1,0:T(8,128)S(1)} all-to-all(f32[8,128,128]{2,1,0:T(8,128)S(1)} %copy.32), channel_id=1, replica_groups=mesh['clique'=8,'shard'=4] {'clique'}, dimensions={0} | all-to-all | bytes 1048576 | tf_op jit(solution)/shard_map/all_to_all | solution.py:55
  304.2 8.8 %gather_fusion.9 = s32[1024]{0:T(1024)} fusion(s32[1024]{0:T(1024)S(1)} %get-tuple-element.24, s32[1024]{0:T(1024)S(1)} %fusion.19), kind=kCustom, calls=%fused_computation.9 | custom fusion | bytes 12288 | tf_op jit(solution)/shard_map/gather | solution.py:22
  313.0 11.5 %all-to-all-done.14 = f32[4,1024,128]{2,1,0:T(8,128)S(1)} async-done(((f32[4,1024,128]{2,1,0:T(8,128)}), f32[4,1024,128]{2,1,0:T(8,128)S(1)}, u32[]{:S(2)}, u32[]{:S(2)}) %all-to-all-start.14) | async-done | bytes 2097184 | tf_op jit(solution)/shard_map/all_to_all | solution.py:42
  335.7 11.4 %all_to_all.124 = f32[4,256,128]{2,1,0:T(8,128)S(1)} all-to-all(f32[4,256,128]{2,1,0:T(8,128)S(1)} %bitcast.101), channel_id=1, replica_groups=mesh['clique'=8,'shard'=4] {'shard'}, dimensions={0} | all-to-all | bytes 1048576 | tf_op jit(solution)/shard_map/all_to_all | solution.py:24
  351.4 9.0 %psum.31 = f32[]{:T(128)} all-reduce(f32[]{:T(128)} %get-tuple-element.40), channel_id=1, replica_groups=mesh['clique'=8,'shard'=4] {'shard'}, use_global_device_ids=true, to_apply=%region_11.12 | all-reduce | flops 1 | bytes 8 | tf_op jit(solution)/shard_map/psum | solution.py:37
  361.1 18.5 %all_to_all.125 = f32[8,128,128]{2,1,0:T(8,128)S(1)} all-to-all(f32[8,128,128]{2,1,0:T(8,128)S(1)} %bitcast.97), channel_id=1, replica_groups=mesh['clique'=8,'shard'=4] {'clique'}, dimensions={0} | all-to-all | bytes 1048576 | tf_op jit(solution)/shard_map/all_to_all | solution.py:52
  380.4 17.7 %all_to_all.126 = f32[8,128,128]{2,1,0:T(8,128)S(1)} all-to-all(f32[8,128,128]{2,1,0:T(8,128)S(1)} %copy.34), channel_id=1, replica_groups=mesh['clique'=8,'shard'=4] {'clique'}, dimensions={0} | all-to-all | bytes 1048576 | tf_op jit(solution)/shard_map/all_to_all | solution.py:55
  403.3 24.7 %all-to-all-done.19 = f32[4,1024,128]{2,1,0:T(8,128)S(1)} async-done(((f32[4,1024,128]{2,1,0:T(8,128)}), f32[4,1024,128]{2,1,0:T(8,128)S(1)}, u32[]{:S(2)}, u32[]{:S(2)}) %all-to-all-start.19) | async-done | bytes 2097184 | tf_op jit(solution)/shard_map/all_to_all | solution.py:42
  (92 shorter events, 114.6 us)
Async XLA Ops:
  13.9 9.9 %all-to-all-start.1 = ((s32[4,1,256]{2,1,0:T(1,128)}), s32[4,1,256]{2,1,0:T(1,128)S(1)}, u32[]{:S(2)}, u32[]{:S(2)}) async-start(s32[4,1,256]{2,1,0:T(1,128)} %bitcast.10), calls=%async_computation.1 | async-start | bytes 8192 | tf_op jit(solution)/shard_map/all_to_all | solution.py:25
  35.0 19.6 %copy-start.7 = (s32[2,8]{1,0:T(2,128)S(1)}, s32[2,8]{1,0:T(2,128)}, u32[]{:S(2)}) copy-start(s32[2,8]{1,0:T(2,128)} %param.7) | copy-start | bytes 196
  39.2 31.6 %copy-start.1 = (f32[1024,128]{1,0:T(8,128)}, f32[1024,128]{1,0:T(8,128)S(1)}, u32[]{:S(2)}) copy-start(f32[1024,128]{1,0:T(8,128)S(1)} %get-tuple-element.35) | copy-start | bytes 1572868
  49.7 20.2 %all-to-all-start.3 = ((f32[8,128,128]{2,1,0:T(8,128)}), f32[8,128,128]{2,1,0:T(8,128)S(1)}, u32[]{:S(2)}, u32[]{:S(2)}) async-start(f32[8,128,128]{2,1,0:T(8,128)} %bitcast.15), calls=%async_computation.3 | async-start | bytes 1048576 | tf_op jit(solution)/shard_map/all_to_all | solution.py:52
  90.1 28.4 %all-to-all-start.5 = ((f32[4,1024,128]{2,1,0:T(8,128)}), f32[4,1024,128]{2,1,0:T(8,128)S(1)}, u32[]{:S(2)}, u32[]{:S(2)}) async-start(f32[4,1024,128]{2,1,0:T(8,128)} %stack.10), calls=%async_computation.5 | async-start | bytes 4194304 | tf_op jit(solution)/shard_map/all_to_all | solution.py:42
  98.1 8.8 %copy-start.5 = (s32[2,1,1024]{2,1,0:T(1,128)S(1)}, s32[2,1,1024]{2,1,0:T(1,128)}, u32[]{:S(2)}) copy-start(s32[2,1,1024]{2,1,0:T(1,128)} %param.6) | copy-start | bytes 24580
  118.5 10.0 %all-to-all-start = ((s32[4,1,256]{2,1,0:T(1,128)}), s32[4,1,256]{2,1,0:T(1,128)S(1)}, u32[]{:S(2)}, u32[]{:S(2)}) async-start(s32[4,1,256]{2,1,0:T(1,128)} %bitcast.4), calls=%async_computation | async-start | bytes 8192 | tf_op jit(solution)/shard_map/all_to_all | solution.py:25
  144.1 29.0 %copy-start.3 = (f32[1024,128]{1,0:T(8,128)}, f32[1024,128]{1,0:T(8,128)S(1)}, u32[]{:S(2)}) copy-start(f32[1024,128]{1,0:T(8,128)S(1)} %get-tuple-element.37) | copy-start | bytes 1572868
  192.5 28.4 %all-to-all-start.9 = ((f32[4,1024,128]{2,1,0:T(8,128)}), f32[4,1024,128]{2,1,0:T(8,128)S(1)}, u32[]{:S(2)}, u32[]{:S(2)}) async-start(f32[4,1024,128]{2,1,0:T(8,128)} %stack.11), calls=%async_computation.9 | async-start | bytes 4194304 | tf_op jit(solution)/shard_map/all_to_all | solution.py:42
  220.8 11.4 %all-to-all-start.10 = ((s32[4,1,256]{2,1,0:T(1,128)}), s32[4,1,256]{2,1,0:T(1,128)S(1)}, u32[]{:S(2)}, u32[]{:S(2)}) async-start(s32[4,1,256]{2,1,0:T(1,128)} %bitcast.32), calls=%async_computation.10 | async-start | bytes 8192 | tf_op jit(solution)/shard_map/all_to_all | solution.py:25
  257.5 37.1 %copy-start.4 = (f32[1024,128]{1,0:T(8,128)S(1)}, f32[1024,128]{1,0:T(8,128)}, u32[]{:S(2)}) copy-start(f32[1024,128]{1,0:T(8,128)} %copy-done.3) | copy-start | bytes 1572868
  296.2 28.4 %all-to-all-start.14 = ((f32[4,1024,128]{2,1,0:T(8,128)}), f32[4,1024,128]{2,1,0:T(8,128)S(1)}, u32[]{:S(2)}, u32[]{:S(2)}) async-start(f32[4,1024,128]{2,1,0:T(8,128)} %stack.12), calls=%async_computation.14 | async-start | bytes 4194304 | tf_op jit(solution)/shard_map/all_to_all | solution.py:42
  304.2 8.8 %copy-start.6 = (s32[2,1,1024]{2,1,0:T(1,128)S(1)}, s32[2,1,1024]{2,1,0:T(1,128)}, u32[]{:S(2)}) copy-start(s32[2,1,1024]{2,1,0:T(1,128)} %param.5) | copy-start | bytes 24580
  324.5 11.2 %all-to-all-start.15 = ((s32[4,1,256]{2,1,0:T(1,128)}), s32[4,1,256]{2,1,0:T(1,128)S(1)}, u32[]{:S(2)}, u32[]{:S(2)}) async-start(s32[4,1,256]{2,1,0:T(1,128)} %bitcast.46), calls=%async_computation.15 | async-start | bytes 8192 | tf_op jit(solution)/shard_map/all_to_all | solution.py:25
  361.1 37.1 %copy-start.2 = (f32[1024,128]{1,0:T(8,128)S(1)}, f32[1024,128]{1,0:T(8,128)}, u32[]{:S(2)}) copy-start(f32[1024,128]{1,0:T(8,128)} %copy-done.1) | copy-start | bytes 1572868
  399.7 28.4 %all-to-all-start.19 = ((f32[4,1024,128]{2,1,0:T(8,128)}), f32[4,1024,128]{2,1,0:T(8,128)S(1)}, u32[]{:S(2)}, u32[]{:S(2)}) async-start(f32[4,1024,128]{2,1,0:T(8,128)} %stack.13), calls=%async_computation.19 | async-start | bytes 4194304 | tf_op jit(solution)/shard_map/all_to_all | solution.py:42
  428.1 4.0 copy-start
